TPU v7x, 128 devices: a whole 4x4x4 slice. The times are simulated.
128 devices in a mesh: group: 8 (over y, core), member: 16 (over z, x).
Axes of the slice: x: 4, y: 4, z: 4, core: 2. Of those that a mesh axis runs over, the one named last changes fastest.
Arguments:
- candidates: bfloat16 [512, 64, 1024], P('member', 'group'), may hold values from -6 to 6
- kv_cache: bfloat16 [64, 2048, 2048], P('group', 'member'), may hold values from -6 to 6
- cache_request: int32 [64], replicated, may hold values from 0 to 63, as said below
- rank_request: int32 [64], replicated, may hold values from 0 to 63, as said below
- hist_blocks: int32 [64], replicated, may hold values from 1 to 16, 544 in all
- w_uq: bfloat16 [1024, 2048], replicated, may hold values from -0.1875 to 0.1875
- w_out: bfloat16 [1024, 1024], replicated, may hold values from -0.1875 to 0.1875
Outputs:
- ranked: bfloat16 [512, 64, 1024], P('member', 'group')
Inputs may be any that keep to these rules, and one draw needn't show every extreme that they name: `cache_request`: A permutation; cache row q lies on group q // 8, events split over member. `rank_request`: A permutation; group g ranks positions g * 8 to (g + 1) * 8 - 1. The requests cached on one group are dealt out to the ranking groups in turn, so every pair of groups carries 8 // 8 or 1 requests and some pair carries exactly 1; the uneven part of the load is the live history lengths.
All inputs are finite; a program needn't handle non-finite values.
Results may differ from a plain program's by a relative error of at most 0.011.
Values may be sent and summed in bfloat16 or wider, within the bound.
No kernel may reach another device: no remote copies, remote signals or barrier semaphores. Data moves between devices by JAX's collectives and lax.ppermute only.
A program may use at most 320 MiB of HBM per device.

v0:
```python
import jax
import jax.numpy as jnp
from jax import lax
from jax.sharding import PartitionSpec as P

HEADS = 8
BLK = 128


def layer_norm(values):
    center = values - jnp.mean(values, axis=-1, keepdims=True)
    spread = jnp.mean(center * center, axis=-1, keepdims=True)
    return center * lax.rsqrt(spread + 1e-05)


def routing(cache_request, rank_request, per_group):
    slot_ids = jnp.arange(cache_request.shape[0], dtype=jnp.int32)
    match = cache_request[:, None] == rank_request[None, :]
    rank_pos = jnp.sum(jnp.where(match, slot_ids[None, :], 0), axis=1)
    target = rank_pos // per_group
    owner_grp = slot_ids // per_group
    earlier = (
        (owner_grp[:, None] == owner_grp[None, :])
        & (target[:, None] == target[None, :])
        & (slot_ids[None, :] < slot_ids[:, None])
    )
    arrival = jnp.sum(earlier.astype(jnp.int32), axis=1)
    slot_of_pos = jnp.sum(jnp.where(match, slot_ids[:, None], 0), axis=0)
    return (target, arrival, slot_of_pos)


def attend_local(queries, piece, live, first_event, scale):
    rows, count = (piece.shape[0], piece.shape[1])
    heads, head_dim = (queries.shape[2], queries.shape[3])
    width = heads * head_dim
    keys = piece[:, :, :width].reshape(rows, count, heads, head_dim)
    values = piece[:, :, width:].reshape(rows, count, heads, head_dim)
    scores = jnp.einsum("rchd,rehd->rhce", queries, keys, preferred_element_type=jnp.float32)
    events = (first_event + jnp.arange(count)).astype(jnp.float32)
    keep = (events[None, :] < live[:, None]).astype(jnp.float32) / live[:, None]
    weights = (jax.nn.silu(scores * scale) * keep[:, None, None, :]).astype(jnp.bfloat16)
    return jnp.einsum("rhce,rehd->rchd", weights, values, preferred_element_type=jnp.float32)


def on_device(candidates, kv_cache, cache_request, rank_request, hist_blocks, w_uq, w_out):
    groups = lax.axis_size("group")
    per_group = kv_cache.shape[0]
    cand_rows = candidates.shape[0]
    width = candidates.shape[2]
    head_dim = width // HEADS
    count = kv_cache.shape[1]
    capacity = (per_group + groups - 1) // groups
    group_now = lax.axis_index("group")
    member_now = lax.axis_index("member")
    target, arrival, slot_of_pos = routing(cache_request, rank_request, per_group)
    first_slot = group_now * per_group
    local_target = lax.dynamic_slice_in_dim(target, first_slot, per_group)
    local_arrival = lax.dynamic_slice_in_dim(arrival, first_slot, per_group)
    row_index = local_target * capacity + local_arrival
    target_grid = jnp.arange(groups)[:, None, None]
    place_grid = jnp.arange(capacity)[None, :, None]
    hits = (local_target[None, None, :] == target_grid) & (
        local_arrival[None, None, :] == place_grid
    )
    chosen = jnp.sum(jnp.where(hits, jnp.arange(per_group)[None, None, :], 0), axis=2).reshape(-1)
    filled = jnp.any(hits, axis=2).reshape(-1)
    positions = first_slot + jnp.arange(per_group)
    source_slot = slot_of_pos[positions]
    receive_index = source_slot // per_group * capacity + arrival[source_slot]
    send_hits = receive_index[None, :] == jnp.arange(groups * capacity)[:, None]
    send_pos = jnp.sum(jnp.where(send_hits, jnp.arange(per_group)[None, :], 0), axis=1)
    send_filled = jnp.any(send_hits, axis=1)
    row_live = (hist_blocks[cache_request[first_slot + jnp.arange(per_group)]] * BLK).astype(
        jnp.float32
    )
    inputs = candidates.astype(jnp.float32)
    normed = layer_norm(inputs).astype(jnp.bfloat16).reshape(cand_rows * per_group, width)
    projected = jax.nn.silu(jnp.dot(normed, w_uq, preferred_element_type=jnp.float32))
    gates = projected[:, :width].reshape(cand_rows, per_group, width)
    queries = projected[:, width:].astype(jnp.bfloat16).reshape(cand_rows, per_group, width)
    scale = head_dim ** (-0.5)
    q_pos = jnp.swapaxes(queries, 0, 1)
    q_out = jnp.where(send_filled[:, None, None], q_pos[send_pos], jnp.zeros((), jnp.bfloat16))
    q_in = lax.all_to_all(q_out, "group", split_axis=0, concat_axis=0, tiled=True)
    q_rows = q_in[row_index]
    q_all = lax.all_gather(q_rows, "member", axis=1, tiled=True)
    q_all = q_all.reshape(per_group, q_all.shape[1], HEADS, head_dim)
    partial = attend_local(q_all, kv_cache, row_live, member_now * count, scale)
    partial = partial.reshape(per_group, partial.shape[1], width)
    summed = lax.psum_scatter(partial, "member", scatter_dimension=1, tiled=True)
    a_out = jnp.where(filled[:, None, None], summed[chosen], jnp.zeros((), jnp.float32))
    a_in = lax.all_to_all(a_out, "group", split_axis=0, concat_axis=0, tiled=True)
    attn = jnp.swapaxes(a_in[receive_index], 0, 1)
    gated = (layer_norm(attn) * gates).astype(jnp.bfloat16).reshape(cand_rows * per_group, width)
    result = jnp.dot(gated, w_out, preferred_element_type=jnp.float32) + inputs.reshape(
        cand_rows * per_group, width
    )
    return result.astype(jnp.bfloat16).reshape(cand_rows, per_group, width)


def solution(mesh):
    return jax.shard_map(
        on_device,
        mesh=mesh,
        in_specs=(P("member", "group", None), P("group", "member", None), P(), P(), P(), P(), P()),
        out_specs=P("member", "group", None),
        check_vma=False,
    )
```

profile of v0, /device:TPU:1, one launch (start us, length us, event | category | flops | bytes accessed | tf_op | source)
XLA Modules:
  0.0 296.7 jit_solution(6112455092179821543)
XLA Ops:
  6.5 0.0 copy-start
  6.5 1.0 fusion.19
  7.6 0.6 gather_fusion
  8.3 0.2 convert_reduce_fusion.1
  8.4 0.6 gather_fusion.1
  9.1 0.1 select_reduce_fusion.1
  9.2 0.1 fusion.21
  9.3 1.2 convert_reduce_fusion
  10.5 0.1 copy.66
  10.6 0.1 copy.67
  10.7 1.3 fusion.5
  12.0 0.1 copy.68
  12.1 0.1 copy.69
  12.2 3.8 %divide_multiply_fusion = f32[256,2048]{1,0:T(8,128)S(1)} fusion(bf16[1024,2048]{1,0:T(8,128)(2,1)} %param.12, bf16[32,8,1024]{2,1,0:T(8,128)(2,1)} %param.7, f32[32,8]{1,0:T(8,128)S(1)} %copy.69, f32[32,8]{1,0:T(8,128)S(1)} %copy.67), kind=kOutput, calls=%fused_computation.10 | convolution fusion | flops 1076887552 | bytes 6817792 | tf_op jit(solution)/shard_map/dot_general | solution.py:78
  16.0 0.0 copy-start.4
  16.0 0.0 copy-start.1
  16.0 0.1 fusion.8
  16.1 0.3 copy.90
  16.4 0.9 copy-done.4
  17.3 0.6 gather_fusion.2
  17.9 0.9 broadcast_select_fusion.1
  18.8 6.0 %all-to-all-start = ((bf16[8,32,1024]{2,1,0:T(8,128)(2,1)}), bf16[8,32,1024]{2,1,0:T(8,128)(2,1)S(1)}, u32[]{:S(2)}, u32[]{:S(2)}) async-start(bf16[8,32,1024]{2,1,0:T(8,128)(2,1)} %broadcast_select_fusion.1), calls=%async_computation | async-start | bytes 1048576 | tf_op jit(solution)/shard_map/all_to_all | solution.py:84
  24.8 0.0 all-gather.3.cloned.1.call-start
  24.8 0.1 compare_select_fusion.5
  24.9 9.3 %all-to-all-done = bf16[8,32,1024]{2,1,0:T(8,128)(2,1)S(1)} async-done(((bf16[8,32,1024]{2,1,0:T(8,128)(2,1)}), bf16[8,32,1024]{2,1,0:T(8,128)(2,1)S(1)}, u32[]{:S(2)}, u32[]{:S(2)}) %all-to-all-start) | async-done | bytes 524320 | tf_op jit(solution)/shard_map/all_to_all | solution.py:84
  34.1 1.4 gather_fusion.3
  35.5 0.0 all-gather.3.cloned.1.call-update
  35.5 0.0 reduce-scatter.2.cloned.1.call-start
  35.6 0.0 copy-done.1
  35.6 0.6 gather_fusion.4
  36.2 4.9 %fusion.33 = (bf16[8,128,1024]{2,1,0:T(8,128)(2,1)}, bf16[8,128,1024]{2,1,0:T(8,128)(2,1)}) fusion(bf16[8,128,2048]{2,1,0:T(8,128)(2,1)} %param.8), kind=kLoop, calls=%fused_computation.101 | loop fusion | bytes 8388608 | tf_op jit(solution)/shard_map/slice | solution.py:36
  41.1 0.0 copy-start.2
  41.1 3.9 %copy.75 = bf16[8,128,1024]{1,2,0:T(8,128)(2,1)} copy(bf16[8,128,1024]{2,1,0:T(8,128)(2,1)} %get-tuple-element.10) | data formatting | bytes 4194304 | tf_op jit(solution)/shard_map/slice | solution.py:37
  45.0 4.0 %copy.81 = bf16[8,128,1024]{1,2,0:T(8,128)(2,1)} copy(bf16[8,128,1024]{2,1,0:T(8,128)(2,1)} %get-tuple-element.9) | data formatting | bytes 4194304
  49.0 0.0 copy-done.2
  49.0 0.6 gather_fusion.5
  49.7 0.1 convert_divide_fusion
  49.8 57.3 %all-gather.3.cloned.1.call-done = bf16[8,512,1024]{2,1,0:T(8,128)(2,1)} async-done(((bf16[8,32,1024]{2,1,0:T(8,128)(2,1)}), bf16[8,512,1024]{2,1,0:T(8,128)(2,1)}) %all-gather.3.cloned.1.call-update) | async-done | bytes 8388624 | tf_op jit(solution)/shard_map/all_gather | solution.py:86
  107.1 11.4 %copy.71 = bf16[8,512,1024]{1,2,0:T(8,128)(2,1)} copy(bf16[8,512,1024]{2,1,0:T(8,128)(2,1)} %all-gather.3.cloned.1.call-done) | data formatting | bytes 16777216 | tf_op jit(solution)/shard_map/all_gather | solution.py:86
  118.5 15.3 %fusion = f32[8,8,512,128]{2,3,1,0:T(8,128)} fusion(bf16[8,128,8,128]{1,3,2,0:T(8,128)(2,1)} %bitcast.74, bf16[8,512,8,128]{1,3,2,0:T(8,128)(2,1)} %bitcast.73, bf16[8,128,8,128]{1,3,2,0:T(8,128)(2,1)} %bitcast.75, f32[8,128]{1,0:T(8,128)S(1)} %convert_divide_fusion), kind=kOutput, calls=%fused_computation.9 | convolution fusion | flops 2176843776 | bytes 29364224 | tf_op jit(solution)/shard_map/rhce,rehd->rchd/dot_general | solution.py:42
  133.8 16.4 %copy.76 = f32[8,512,1024]{2,1,0:T(8,128)} copy(f32[8,512,1024]{1,2,0:T(8,128)} %bitcast.72) | data formatting | bytes 33554432 | tf_op jit(solution)/shard_map/reshape | solution.py:89
  150.2 0.0 reduce-scatter.2.cloned.1.call-update
  150.2 0.1 broadcast_compare_fusion
  150.3 0.1 select_reduce_fusion
  150.4 0.1 fusion.23
  150.5 110.2 %reduce-scatter.2.cloned.1.call-done = f32[8,32,1024]{2,1,0:T(8,128)} async-done(((f32[8,512,1024]{2,1,0:T(8,128)}), f32[8,32,1024]{2,1,0:T(8,128)}) %reduce-scatter.2.cloned.1.call-update) | async-done | bytes 1048592 | tf_op jit(solution)/shard_map/reduce_scatter | solution.py:90
  260.7 1.8 gather_fusion.6
  262.6 1.2 broadcast_select_fusion
  263.7 5.2 %all-to-all-start.1 = ((f32[8,32,1024]{2,1,0:T(8,128)}), f32[8,32,1024]{2,1,0:T(8,128)}, u32[]{:S(2)}, u32[]{:S(2)}) async-start(f32[8,32,1024]{2,1,0:T(8,128)} %broadcast_select_fusion), calls=%async_computation.2 | async-start | bytes 2097152 | tf_op jit(solution)/shard_map/all_to_all | solution.py:92
  269.0 2.4 slice_bitcast_fusion
  271.3 12.7 %all-to-all-done.1 = f32[8,32,1024]{2,1,0:T(8,128)} async-done(((f32[8,32,1024]{2,1,0:T(8,128)}), f32[8,32,1024]{2,1,0:T(8,128)}, u32[]{:S(2)}, u32[]{:S(2)}) %all-to-all-start.1) | async-done | bytes 1048608 | tf_op jit(solution)/shard_map/all_to_all | solution.py:92
  284.0 1.8 gather_fusion.7
  285.9 0.0 copy-start.3
  285.9 0.1 bitcast_reduce_fusion
  286.0 0.2 multiply_reduce_fusion
  286.3 1.9 fusion.7
  288.2 0.0 copy-done
  288.2 0.0 copy-done.3
  288.2 1.6 fusion.4
  (21 shorter events, 0.1 us)
Async XLA Ops:
  6.5 281.6 %copy-start = (bf16[1024,1024]{1,0:T(8,128)(2,1)S(1)}, bf16[1024,1024]{1,0:T(8,128)(2,1)}, u32[]{:S(2)}) copy-start(bf16[1024,1024]{1,0:T(8,128)(2,1)} %param.13) | copy-start | bytes 6291460
  16.0 1.3 copy-start.4
  16.0 19.6 %copy-start.1 = (s32[64]{0:T(128)S(1)}, s32[64]{0:T(128)}, u32[]{:S(2)}) copy-start(s32[64]{0:T(128)} %param.9) | copy-start | bytes 772
  18.8 15.3 %all-to-all-start = ((bf16[8,32,1024]{2,1,0:T(8,128)(2,1)}), bf16[8,32,1024]{2,1,0:T(8,128)(2,1)S(1)}, u32[]{:S(2)}, u32[]{:S(2)}) async-start(bf16[8,32,1024]{2,1,0:T(8,128)(2,1)} %broadcast_select_fusion.1), calls=%async_computation | async-start | bytes 1048576 | tf_op jit(solution)/shard_map/all_to_all | solution.py:84
  24.8 82.3 %all-gather.3.cloned.1.call-start = ((), (), s32[]{:S(2)}) async-start(), calls=%async_computation.4 | async-start | bytes 8912896 | tf_op jit(solution)/shard_map/all_gather | solution.py:86
  35.5 225.2 %reduce-scatter.2.cloned.1.call-start = ((), (), s32[]{:S(2)}) async-start(), calls=%async_computation.3 | async-start | bytes 17825792 | tf_op jit(solution)/shard_map/reduce_scatter | solution.py:90
  41.1 7.9 %copy-start.2 = (s32[64]{0:T(128)S(1)}, s32[64]{0:T(128)}, u32[]{:S(2)}) copy-start(s32[64]{0:T(128)} %param.11) | copy-start | bytes 772
  263.7 20.3 %all-to-all-start.1 = ((f32[8,32,1024]{2,1,0:T(8,128)}), f32[8,32,1024]{2,1,0:T(8,128)}, u32[]{:S(2)}, u32[]{:S(2)}) async-start(f32[8,32,1024]{2,1,0:T(8,128)} %broadcast_select_fusion), calls=%async_computation.2 | async-start | bytes 2097152 | tf_op jit(solution)/shard_map/all_to_all | solution.py:92
  285.9 2.3 copy-start.3
Sparse Core Ops, SparseCore 0:
  35.6 71.4 all-gather.2
  150.3 110.3 reduce-scatter.1
where the time goes:
time: 298 us; the launch traced here: 297 us
  waiting for transfers between devices  189 us (63%)
  local copies, waits for them, and re-layouts  52.7 us (18%)
  matrix products  20.7 us (7%)
  between operations  13.6 us (5%)
  starting transfers between devices  11.2 us (4%)
  other arithmetic  8.88 us (3%)
    reduce_scatter x1, waiting for transfers between devices, on_device(): lax.psum_scatter(partial, 'member', scatter_dimension=1, tiled=True)  110 us
    all_gather x1, waiting for transfers between devices, on_device(): q_all = lax.all_gather(q_rows, 'member', axis=1, tiled=True)  57.3 us
    reshape x1, local copies, waits for them, and re-layouts, on_device(): partial = partial.reshape(per_group, partial.shape[1], width)  16.4 us
    dot_general x1, matrix products, attend_local(): jnp.einsum('rhce,rehd->rchd', weights, values, preferred_element_type=jnp...  15.3 us
    all_to_all x1, waiting for transfers between devices, on_device(): lax.all_to_all(a_out, 'group', split_axis=0, concat_axis=0, tiled=True)  12.7 us
    all_gather x1, local copies, waits for them, and re-layouts, on_device(): q_all = lax.all_gather(q_rows, 'member', axis=1, tiled=True)  11.4 us
    all_to_all x1, waiting for transfers between devices, on_device(): lax.all_to_all(q_out, 'group', split_axis=0, concat_axis=0, tiled=True)  9.26 us
  transfers between devices with their start and end apart: 4, of which 4 were waited for; matrix products, arithmetic and copies ran while one was open for 6% of the time, Pallas kernels for 0%

commit v1 on v0

--- a/solution.py
+++ b/solution.py
@@ -83,7 +83,25 @@
     q_out = jnp.where(send_filled[:, None, None], q_pos[send_pos], jnp.zeros((), jnp.bfloat16))
     q_in = lax.all_to_all(q_out, "group", split_axis=0, concat_axis=0, tiled=True)
     q_rows = q_in[row_index]
-    q_all = lax.all_gather(q_rows, "member", axis=1, tiled=True)
+    opened = lax.axis_index("member")
+    prior = lax.axis_size("member")
+    after, part_next, a_next = (prior, opened, q_rows.shape[1])
+    samples = [(no, (no + 1) % after) for no in range(after)]
+    q_all = jnp.zeros((*q_rows.shape[:1], after * a_next, *q_rows.shape[1 + 1 :]), q_rows.dtype)
+    fields = [(no, (no - 1) % after) for no in range(after)]
+    tmp = mixed_arr = q_rows
+    base_arr = after // 2
+    q_all = lax.dynamic_update_slice_in_dim(q_all, q_rows, part_next * a_next, axis=1)
+    for k in range(1, base_arr + 1):
+        tmp = lax.ppermute(tmp, axis_name="member", perm=samples)
+        q_all = lax.dynamic_update_slice_in_dim(
+            q_all, tmp, (part_next - k) % after * a_next, axis=1
+        )
+        if k < after - base_arr:
+            mixed_arr = lax.ppermute(mixed_arr, axis_name="member", perm=fields)
+            q_all = lax.dynamic_update_slice_in_dim(
+                q_all, mixed_arr, (part_next + k) % after * a_next, axis=1
+            )
     q_all = q_all.reshape(per_group, q_all.shape[1], HEADS, head_dim)
     partial = attend_local(q_all, kv_cache, row_live, member_now * count, scale)
     partial = partial.reshape(per_group, partial.shape[1], width)

time: 298 us -> 735 us (2.47); the launches traced: 297 us -> 725 us
  local copies, waits for them, and re-layouts: 52.7 us -> 442 us
  starting transfers between devices: 11.2 us -> 46.1 us
    dynamic_update_slice x0 -> x16, local copies, waits for them, and re-layouts: none -> 364 us  [the longest x8 180 us: on_device(): lax.dynamic_update_slice_in_dim(q_all, tmp, (part_next - k) % after * a_n...]
    all_gather x1 -> x0, waiting for transfers between devices: 57.3 us -> none  [on_device(): q_all = lax.all_gather(q_rows, 'member', axis=1, tiled=True)]
    ppermute x0 -> x15, waiting for transfers between devices: none -> 55.1 us  [the longest x8 55.1 us: on_device(): tmp = lax.ppermute(tmp, axis_name='member', perm=samples)]
    ppermute x0 -> x15, starting transfers between devices: none -> 34.9 us  [the longest x7 33.5 us: on_device(): mixed_arr = lax.ppermute(mixed_arr, axis_name='member', perm=fields)]
    ppermute x0 -> x15, local copies, waits for them, and re-layouts: none -> 31.2 us  [the longest x8 16.5 us: on_device(): tmp = lax.ppermute(tmp, axis_name='member', perm=samples)]
    all_gather x1 -> x0, local copies, waits for them, and re-layouts: 11.4 us -> none  [on_device(): q_all = lax.all_gather(q_rows, 'member', axis=1, tiled=True)]
  transfers between devices with their start and end apart: 4 -> 18, of which waited for: 4 -> 9; matrix products, arithmetic and copies ran while one was open for 6% -> 54% of each run, Pallas kernels for 0% -> 0%
where the time goes in v1:
time: 735 us; the launch traced here: 725 us
  local copies, waits for them, and re-layouts  442 us (60%)
  waiting for transfers between devices  194 us (26%)
  starting transfers between devices  46.1 us (6%)
  matrix products  20.7 us (3%)
  between operations  13.8 us (2%)
  other arithmetic  8.86 us (1%)
    dynamic_update_slice x8, local copies, waits for them, and re-layouts, on_device(): lax.dynamic_update_slice_in_dim(q_all, tmp, (part_next - k) % after * a_n...  180 us
    dynamic_update_slice x7, local copies, waits for them, and re-layouts, on_device(): lax.dynamic_update_slice_in_dim(q_all, mixed_arr, (part_next + k) % after...  163 us
    reduce_scatter x1, waiting for transfers between devices, on_device(): lax.psum_scatter(partial, 'member', scatter_dimension=1, tiled=True)  117 us
    ppermute x8, waiting for transfers between devices, on_device(): tmp = lax.ppermute(tmp, axis_name='member', perm=samples)  55.1 us
    ppermute x7, starting transfers between devices, on_device(): mixed_arr = lax.ppermute(mixed_arr, axis_name='member', perm=fields)  33.5 us
    dynamic_update_slice x1, local copies, waits for them, and re-layouts, on_device(): lax.dynamic_update_slice_in_dim(q_all, q_rows, part_next * a_next, axis=1)  20.5 us
    ppermute x8, local copies, waits for them, and re-layouts, on_device(): tmp = lax.ppermute(tmp, axis_name='member', perm=samples)  16.5 us
    reshape x1, local copies, waits for them, and re-layouts, on_device(): partial = partial.reshape(per_group, partial.shape[1], width)  16.4 us
  transfers between devices with their start and end apart: 18, of which 9 were waited for; matrix products, arithmetic and copies ran while one was open for 54% of the time, Pallas kernels for 0%

profile of v1, /device:TPU:1, one launch (start us, length us, event | category | flops | bytes accessed | tf_op | source)
XLA Modules:
  0.0 725.0 jit_solution(16052318051658382764)
XLA Ops:
  10.7 1.3 fusion.5
  12.2 3.8 divide_multiply_fusion
  18.8 6.0 all-to-all-start
  24.9 9.3 %all-to-all-done = bf16[8,32,1024]{2,1,0:T(8,128)(2,1)S(1)} async-done(((bf16[8,32,1024]{2,1,0:T(8,128)(2,1)}), bf16[8,32,1024]{2,1,0:T(8,128)(2,1)S(1)}, u32[]{:S(2)}, u32[]{:S(2)}) %all-to-all-start) | async-done | bytes 524320 | tf_op jit(solution)/shard_map/all_to_all | solution.py:84
  34.7 1.3 collective-permute-start
  36.0 4.8 collective-permute-start.1
  40.8 11.2 %collective-permute-done = bf16[8,32,1024]{2,1,0:T(8,128)(2,1)S(1)} collective-permute-done((bf16[8,32,1024]{2,1,0:T(8,128)(2,1)S(1)}, bf16[8,32,1024]{2,1,0:T(8,128)(2,1)S(1)}, u32[]{:S(2)}, u32[]{:S(2)}) %collective-permute-start) | collective-permute-done | bytes 524320 | tf_op jit(solution)/shard_map/ppermute | solution.py:96
  52.1 4.8 collective-permute-start.3
  56.9 10.5 %collective-permute-done.2 = bf16[8,32,1024]{2,1,0:T(8,128)(2,1)S(1)} collective-permute-done((bf16[8,32,1024]{2,1,0:T(8,128)(2,1)S(1)}, bf16[8,32,1024]{2,1,0:T(8,128)(2,1)S(1)}, u32[]{:S(2)}, u32[]{:S(2)}) %collective-permute-start.2) | collective-permute-done | bytes 524320 | tf_op jit(solution)/shard_map/ppermute | solution.py:96
  67.4 4.8 collective-permute-start.5
  72.1 9.6 %collective-permute-done.4 = bf16[8,32,1024]{2,1,0:T(8,128)(2,1)S(1)} collective-permute-done((bf16[8,32,1024]{2,1,0:T(8,128)(2,1)S(1)}, bf16[8,32,1024]{2,1,0:T(8,128)(2,1)S(1)}, u32[]{:S(2)}, u32[]{:S(2)}) %collective-permute-start.4) | collective-permute-done | bytes 524320 | tf_op jit(solution)/shard_map/ppermute | solution.py:96
  81.8 4.8 collective-permute-start.7
  86.5 8.8 %collective-permute-done.6 = bf16[8,32,1024]{2,1,0:T(8,128)(2,1)S(1)} collective-permute-done((bf16[8,32,1024]{2,1,0:T(8,128)(2,1)S(1)}, bf16[8,32,1024]{2,1,0:T(8,128)(2,1)S(1)}, u32[]{:S(2)}, u32[]{:S(2)}) %collective-permute-start.6) | collective-permute-done | bytes 524320 | tf_op jit(solution)/shard_map/ppermute | solution.py:96
  95.3 4.8 collective-permute-start.9
  100.1 7.9 %collective-permute-done.8 = bf16[8,32,1024]{2,1,0:T(8,128)(2,1)S(1)} collective-permute-done((bf16[8,32,1024]{2,1,0:T(8,128)(2,1)S(1)}, bf16[8,32,1024]{2,1,0:T(8,128)(2,1)S(1)}, u32[]{:S(2)}, u32[]{:S(2)}) %collective-permute-start.8) | collective-permute-done | bytes 524320 | tf_op jit(solution)/shard_map/ppermute | solution.py:96
  108.0 4.8 collective-permute-start.11
  112.8 7.1 collective-permute-done.10
  120.1 4.9 fusion.33
  125.6 3.9 copy.165
  129.5 3.9 copy.171
  134.1 4.8 collective-permute-start.13
  139.0 1.7 copy.146
  140.7 3.9 broadcast_in_dim.74
  144.7 20.5 %dynamic_update_slice.48 = bf16[8,512,1024]{1,2,0:T(8,128)(2,1)} dynamic-update-slice(bf16[8,512,1024]{1,2,0:T(8,128)(2,1)} %broadcast_in_dim.74, bf16[8,32,1024]{1,2,0:T(8,128)(2,1)} %copy.146, s32[]{:T(128)} %constant.143.clone.1, s32[]{:T(128)S(6)} %select_n.265, s32[]{:T(128)} %constant.143.clone.1) | dynamic-update-slice | bytes 1048580 | tf_op jit(solution)/shard_map/dynamic_update_slice | solution.py:94
  165.2 2.7 copy.147
  167.8 22.9 %dynamic_update_slice.49 = bf16[8,512,1024]{1,2,0:T(8,128)(2,1)} dynamic-update-slice(bf16[8,512,1024]{1,2,0:T(8,128)(2,1)} %dynamic_update_slice.48, bf16[8,32,1024]{1,2,0:T(8,128)(2,1)} %copy.147, s32[]{:T(128)} %constant.143.clone.1, s32[]{:T(128)S(6)} %select_n.267, s32[]{:T(128)} %constant.143.clone.1) | dynamic-update-slice | bytes 1048580 | tf_op jit(solution)/shard_map/dynamic_update_slice | solution.py:97
  190.8 1.7 copy.148
  192.5 23.8 %dynamic_update_slice.50 = bf16[8,512,1024]{1,2,0:T(8,128)(2,1)} dynamic-update-slice(bf16[8,512,1024]{1,2,0:T(8,128)(2,1)} %dynamic_update_slice.49, bf16[8,32,1024]{1,2,0:T(8,128)(2,1)} %copy.148, s32[]{:T(128)} %constant.143.clone.1, s32[]{:T(128)S(6)} %select_n.269, s32[]{:T(128)} %constant.143.clone.1) | dynamic-update-slice | bytes 1048580 | tf_op jit(solution)/shard_map/dynamic_update_slice | solution.py:102
  216.3 1.7 copy.149
  218.0 23.0 %dynamic_update_slice.51 = bf16[8,512,1024]{1,2,0:T(8,128)(2,1)} dynamic-update-slice(bf16[8,512,1024]{1,2,0:T(8,128)(2,1)} %dynamic_update_slice.50, bf16[8,32,1024]{1,2,0:T(8,128)(2,1)} %copy.149, s32[]{:T(128)} %constant.143.clone.1, s32[]{:T(128)S(6)} %select_n.271, s32[]{:T(128)} %constant.143.clone.1) | dynamic-update-slice | bytes 1048580 | tf_op jit(solution)/shard_map/dynamic_update_slice | solution.py:97
  241.1 1.7 copy.150
  242.8 23.8 %dynamic_update_slice.52 = bf16[8,512,1024]{1,2,0:T(8,128)(2,1)} dynamic-update-slice(bf16[8,512,1024]{1,2,0:T(8,128)(2,1)} %dynamic_update_slice.51, bf16[8,32,1024]{1,2,0:T(8,128)(2,1)} %copy.150, s32[]{:T(128)} %constant.143.clone.1, s32[]{:T(128)S(6)} %select_n.273, s32[]{:T(128)} %constant.143.clone.1) | dynamic-update-slice | bytes 1048580 | tf_op jit(solution)/shard_map/dynamic_update_slice | solution.py:102
  266.6 1.7 copy.151
  268.3 23.0 %dynamic_update_slice.53 = bf16[8,512,1024]{1,2,0:T(8,128)(2,1)} dynamic-update-slice(bf16[8,512,1024]{1,2,0:T(8,128)(2,1)} %dynamic_update_slice.52, bf16[8,32,1024]{1,2,0:T(8,128)(2,1)} %copy.151, s32[]{:T(128)} %constant.143.clone.1, s32[]{:T(128)S(6)} %select_n.275, s32[]{:T(128)} %constant.143.clone.1) | dynamic-update-slice | bytes 1048580 | tf_op jit(solution)/shard_map/dynamic_update_slice | solution.py:97
  291.3 1.7 copy.152
  293.1 23.8 %dynamic_update_slice.54 = bf16[8,512,1024]{1,2,0:T(8,128)(2,1)} dynamic-update-slice(bf16[8,512,1024]{1,2,0:T(8,128)(2,1)} %dynamic_update_slice.53, bf16[8,32,1024]{1,2,0:T(8,128)(2,1)} %copy.152, s32[]{:T(128)} %constant.143.clone.1, s32[]{:T(128)S(6)} %select_n.277, s32[]{:T(128)} %constant.143.clone.1) | dynamic-update-slice | bytes 1048580 | tf_op jit(solution)/shard_map/dynamic_update_slice | solution.py:102
  316.9 1.7 copy.153
  318.6 19.6 %dynamic_update_slice.55 = bf16[8,512,1024]{1,2,0:T(8,128)(2,1)} dynamic-update-slice(bf16[8,512,1024]{1,2,0:T(8,128)(2,1)} %dynamic_update_slice.54, bf16[8,32,1024]{1,2,0:T(8,128)(2,1)} %copy.153, s32[]{:T(128)} %constant.143.clone.1, s32[]{:T(128)S(6)} %select_n.279, s32[]{:T(128)} %constant.143.clone.1) | dynamic-update-slice | bytes 1048580 | tf_op jit(solution)/shard_map/dynamic_update_slice | solution.py:97
  338.2 1.7 copy.154
  340.0 20.5 %dynamic_update_slice.56 = bf16[8,512,1024]{1,2,0:T(8,128)(2,1)} dynamic-update-slice(bf16[8,512,1024]{1,2,0:T(8,128)(2,1)} %dynamic_update_slice.55, bf16[8,32,1024]{1,2,0:T(8,128)(2,1)} %copy.154, s32[]{:T(128)} %constant.143.clone.1, s32[]{:T(128)S(6)} %select_n.281, s32[]{:T(128)} %constant.143.clone.1) | dynamic-update-slice | bytes 1048580 | tf_op jit(solution)/shard_map/dynamic_update_slice | solution.py:102
  360.5 1.7 copy.155
  362.2 23.8 %dynamic_update_slice.57 = bf16[8,512,1024]{1,2,0:T(8,128)(2,1)} dynamic-update-slice(bf16[8,512,1024]{1,2,0:T(8,128)(2,1)} %dynamic_update_slice.56, bf16[8,32,1024]{1,2,0:T(8,128)(2,1)} %copy.155, s32[]{:T(128)} %constant.143.clone.1, s32[]{:T(128)S(6)} %select_n.283, s32[]{:T(128)} %constant.143.clone.1) | dynamic-update-slice | bytes 1048580 | tf_op jit(solution)/shard_map/dynamic_update_slice | solution.py:97
  386.0 2.6 copy.156
  388.6 23.8 %dynamic_update_slice.58 = bf16[8,512,1024]{1,2,0:T(8,128)(2,1)} dynamic-update-slice(bf16[8,512,1024]{1,2,0:T(8,128)(2,1)} %dynamic_update_slice.57, bf16[8,32,1024]{1,2,0:T(8,128)(2,1)} %copy.156, s32[]{:T(128)} %constant.143.clone.1, s32[]{:T(128)S(6)} %select_n.285, s32[]{:T(128)} %constant.143.clone.1) | dynamic-update-slice | bytes 1048580 | tf_op jit(solution)/shard_map/dynamic_update_slice | solution.py:102
  412.3 2.6 copy.157
  415.0 23.8 %dynamic_update_slice.59 = bf16[8,512,1024]{1,2,0:T(8,128)(2,1)} dynamic-update-slice(bf16[8,512,1024]{1,2,0:T(8,128)(2,1)} %dynamic_update_slice.58, bf16[8,32,1024]{1,2,0:T(8,128)(2,1)} %copy.157, s32[]{:T(128)} %constant.143.clone.1, s32[]{:T(128)S(6)} %select_n.287, s32[]{:T(128)} %constant.143.clone.1) | dynamic-update-slice | bytes 1048580 | tf_op jit(solution)/shard_map/dynamic_update_slice | solution.py:97
  438.7 2.6 copy.158
  441.3 23.8 %dynamic_update_slice.60 = bf16[8,512,1024]{1,2,0:T(8,128)(2,1)} dynamic-update-slice(bf16[8,512,1024]{1,2,0:T(8,128)(2,1)} %dynamic_update_slice.59, bf16[8,32,1024]{1,2,0:T(8,128)(2,1)} %copy.158, s32[]{:T(128)} %constant.143.clone.1, s32[]{:T(128)S(6)} %select_n.289, s32[]{:T(128)} %constant.143.clone.1) | dynamic-update-slice | bytes 1048580 | tf_op jit(solution)/shard_map/dynamic_update_slice | solution.py:102
  465.1 1.7 copy.159
  466.8 23.8 %dynamic_update_slice.61 = bf16[8,512,1024]{1,2,0:T(8,128)(2,1)} dynamic-update-slice(bf16[8,512,1024]{1,2,0:T(8,128)(2,1)} %dynamic_update_slice.60, bf16[8,32,1024]{1,2,0:T(8,128)(2,1)} %copy.159, s32[]{:T(128)} %constant.143.clone.1, s32[]{:T(128)S(6)} %select_n.291, s32[]{:T(128)} %constant.143.clone.1) | dynamic-update-slice | bytes 1048580 | tf_op jit(solution)/shard_map/dynamic_update_slice | solution.py:97
  490.6 2.6 copy.160
  493.2 23.8 %dynamic_update_slice.62 = bf16[8,512,1024]{1,2,0:T(8,128)(2,1)} dynamic-update-slice(bf16[8,512,1024]{1,2,0:T(8,128)(2,1)} %dynamic_update_slice.61, bf16[8,32,1024]{1,2,0:T(8,128)(2,1)} %copy.160, s32[]{:T(128)} %constant.143.clone.1, s32[]{:T(128)S(6)} %select_n.293, s32[]{:T(128)} %constant.143.clone.1) | dynamic-update-slice | bytes 1048580 | tf_op jit(solution)/shard_map/dynamic_update_slice | solution.py:102
  517.0 2.6 copy.161
  519.6 20.5 %dynamic_update_slice.63 = bf16[8,512,1024]{1,2,0:T(8,128)(2,1)} dynamic-update-slice(bf16[8,512,1024]{1,2,0:T(8,128)(2,1)} %dynamic_update_slice.62, bf16[8,32,1024]{1,2,0:T(8,128)(2,1)} %copy.161, s32[]{:T(128)} %constant.143.clone.1, s32[]{:T(128)S(6)} %select_n.295, s32[]{:T(128)} %constant.143.clone.1) | dynamic-update-slice | bytes 1048580 | tf_op jit(solution)/shard_map/dynamic_update_slice | solution.py:97
  540.1 15.3 %fusion = f32[8,8,512,128]{2,3,1,0:T(8,128)} fusion(bf16[8,128,8,128]{1,3,2,0:T(8,128)(2,1)} %bitcast.74, bf16[8,512,8,128]{1,3,2,0:T(8,128)(2,1)} %bitcast.73, bf16[8,128,8,128]{1,3,2,0:T(8,128)(2,1)} %bitcast.75, f32[8,128]{1,0:T(8,128)S(1)} %convert_divide_fusion), kind=kOutput, calls=%fused_computation.9 | convolution fusion | flops 2176843776 | bytes 29364224 | tf_op jit(solution)/shard_map/rhce,rehd->rchd/dot_general | solution.py:42
  555.3 16.4 %copy.166 = f32[8,512,1024]{2,1,0:T(8,128)} copy(f32[8,512,1024]{1,2,0:T(8,128)} %bitcast.72) | data formatting | bytes 33554432 | tf_op jit(solution)/shard_map/reshape | solution.py:107
  572.1 116.9 %reduce-scatter.2.cloned.1.call-done = f32[8,32,1024]{2,1,0:T(8,128)} async-done(((f32[8,512,1024]{2,1,0:T(8,128)}), f32[8,32,1024]{2,1,0:T(8,128)}) %reduce-scatter.2.cloned.1.call-update) | async-done | bytes 1048592 | tf_op jit(solution)/shard_map/reduce_scatter | solution.py:108
  689.0 1.8 gather_fusion.6
  692.0 5.3 all-to-all-start.1
  697.3 2.3 slice_bitcast_fusion
  699.6 12.7 %all-to-all-done.1 = f32[8,32,1024]{2,1,0:T(8,128)} async-done(((f32[8,32,1024]{2,1,0:T(8,128)}), f32[8,32,1024]{2,1,0:T(8,128)}, u32[]{:S(2)}, u32[]{:S(2)}) %all-to-all-start.1) | async-done | bytes 1048608 | tf_op jit(solution)/shard_map/all_to_all | solution.py:110
  712.3 1.8 gather_fusion.7
  714.6 1.9 fusion.7
  716.5 1.6 fusion.4
  (109 shorter events, 11.2 us)
Async XLA Ops:
  6.5 710.0 %copy-start = (bf16[1024,1024]{1,0:T(8,128)(2,1)S(1)}, bf16[1024,1024]{1,0:T(8,128)(2,1)}, u32[]{:S(2)}) copy-start(bf16[1024,1024]{1,0:T(8,128)(2,1)} %param.13) | copy-start | bytes 6291460
  16.0 1.3 copy-start.4
  18.8 15.3 %all-to-all-start = ((bf16[8,32,1024]{2,1,0:T(8,128)(2,1)}), bf16[8,32,1024]{2,1,0:T(8,128)(2,1)S(1)}, u32[]{:S(2)}, u32[]{:S(2)}) async-start(bf16[8,32,1024]{2,1,0:T(8,128)(2,1)} %broadcast_select_fusion.1), calls=%async_computation | async-start | bytes 1048576 | tf_op jit(solution)/shard_map/all_to_all | solution.py:84
  24.8 664.2 %reduce-scatter.2.cloned.1.call-start = ((), (), s32[]{:S(2)}) async-start(), calls=%async_computation.3 | async-start | bytes 17825792 | tf_op jit(solution)/shard_map/reduce_scatter | solution.py:108
  34.7 90.2 %copy-start.1 = (s32[64]{0:T(128)S(1)}, s32[64]{0:T(128)}, u32[]{:S(2)}) copy-start(s32[64]{0:T(128)} %param.9) | copy-start | bytes 772
  34.7 17.4 %collective-permute-start = (bf16[8,32,1024]{2,1,0:T(8,128)(2,1)S(1)}, bf16[8,32,1024]{2,1,0:T(8,128)(2,1)S(1)}, u32[]{:S(2)}, u32[]{:S(2)}) collective-permute-start(bf16[8,32,1024]{2,1,0:T(8,128)(2,1)S(1)} %gather_fusion.3), channel_id=1, source_target_pairs={{0,1},{1,2},{2,3},{3,4},{4,5},{5,6},{6,7},{7,8},{8,9},{9,10},{10,1... | collective-permute-start | bytes 1572872 | tf_op jit(solution)/shard_map/ppermute | solution.py:96
  36.0 16.1 %collective-permute-start.1 = (bf16[8,32,1024]{2,1,0:T(8,128)(2,1)S(1)}, bf16[8,32,1024]{2,1,0:T(8,128)(2,1)S(1)}, u32[]{:S(2)}, u32[]{:S(2)}) collective-permute-start(bf16[8,32,1024]{2,1,0:T(8,128)(2,1)S(1)} %gather_fusion.3), channel_id=1, source_target_pairs={{0,15},{1,0},{2,1},{3,2},{4,3},{5,4},{6,5},{7,6},{8,7},{9,8},{10,9... | collective-permute-start | bytes 1572872 | tf_op jit(solution)/shard_map/ppermute | solution.py:101
  52.1 67.8 %copy-start.9 = (bf16[8,32,1024]{2,1,0:T(8,128)(2,1)}, bf16[8,32,1024]{2,1,0:T(8,128)(2,1)S(1)}, u32[]{:S(2)}) copy-start(bf16[8,32,1024]{2,1,0:T(8,128)(2,1)S(1)} %collective-permute-done) | copy-start | bytes 1572868
  52.1 15.3 %collective-permute-start.2 = (bf16[8,32,1024]{2,1,0:T(8,128)(2,1)S(1)}, bf16[8,32,1024]{2,1,0:T(8,128)(2,1)S(1)}, u32[]{:S(2)}, u32[]{:S(2)}) collective-permute-start(bf16[8,32,1024]{2,1,0:T(8,128)(2,1)S(1)} %collective-permute-done), channel_id=1, source_target_pairs={{0,1},{1,2},{2,3},{3,4},{4,5},{5,6},{6,7},{7,8},{8,9},{9,10},{10,1... | collective-permute-start | bytes 1572872 | tf_op jit(solution)/shard_map/ppermute | solution.py:96
  52.1 60.7 %copy-start.5 = (bf16[8,32,1024]{2,1,0:T(8,128)(2,1)}, bf16[8,32,1024]{2,1,0:T(8,128)(2,1)S(1)}, u32[]{:S(2)}) copy-start(bf16[8,32,1024]{2,1,0:T(8,128)(2,1)S(1)} %collective-permute-done.1) | copy-start | bytes 1572868
  52.1 15.2 %collective-permute-start.3 = (bf16[8,32,1024]{2,1,0:T(8,128)(2,1)S(1)}, bf16[8,32,1024]{2,1,0:T(8,128)(2,1)S(1)}, u32[]{:S(2)}, u32[]{:S(2)}) collective-permute-start(bf16[8,32,1024]{2,1,0:T(8,128)(2,1)S(1)} %collective-permute-done.1), channel_id=1, source_target_pairs={{0,15},{1,0},{2,1},{3,2},{4,3},{5,4},{6,5},{7,6},{8,7},{9,8},{10,9... | collective-permute-start | bytes 1572872 | tf_op jit(solution)/shard_map/ppermute | solution.py:101
  67.3 52.6 %copy-start.7 = (bf16[8,32,1024]{2,1,0:T(8,128)(2,1)}, bf16[8,32,1024]{2,1,0:T(8,128)(2,1)S(1)}, u32[]{:S(2)}) copy-start(bf16[8,32,1024]{2,1,0:T(8,128)(2,1)S(1)} %collective-permute-done.2) | copy-start | bytes 1572868
  67.3 14.4 %collective-permute-start.4 = (bf16[8,32,1024]{2,1,0:T(8,128)(2,1)S(1)}, bf16[8,32,1024]{2,1,0:T(8,128)(2,1)S(1)}, u32[]{:S(2)}, u32[]{:S(2)}) collective-permute-start(bf16[8,32,1024]{2,1,0:T(8,128)(2,1)S(1)} %collective-permute-done.2), channel_id=1, source_target_pairs={{0,1},{1,2},{2,3},{3,4},{4,5},{5,6},{6,7},{7,8},{8,9},{9,10},{10,1... | collective-permute-start | bytes 1572872 | tf_op jit(solution)/shard_map/ppermute | solution.py:96
  67.3 52.6 %copy-start.10 = (bf16[8,32,1024]{2,1,0:T(8,128)(2,1)}, bf16[8,32,1024]{2,1,0:T(8,128)(2,1)S(1)}, u32[]{:S(2)}) copy-start(bf16[8,32,1024]{2,1,0:T(8,128)(2,1)S(1)} %collective-permute-done.3) | copy-start | bytes 1572868
  67.4 14.4 %collective-permute-start.5 = (bf16[8,32,1024]{2,1,0:T(8,128)(2,1)S(1)}, bf16[8,32,1024]{2,1,0:T(8,128)(2,1)S(1)}, u32[]{:S(2)}, u32[]{:S(2)}) collective-permute-start(bf16[8,32,1024]{2,1,0:T(8,128)(2,1)S(1)} %collective-permute-done.3), channel_id=1, source_target_pairs={{0,15},{1,0},{2,1},{3,2},{4,3},{5,4},{6,5},{7,6},{8,7},{9,8},{10,9... | collective-permute-start | bytes 1572872 | tf_op jit(solution)/shard_map/ppermute | solution.py:101
  81.7 38.2 %copy-start.12 = (bf16[8,32,1024]{2,1,0:T(8,128)(2,1)}, bf16[8,32,1024]{2,1,0:T(8,128)(2,1)S(1)}, u32[]{:S(2)}) copy-start(bf16[8,32,1024]{2,1,0:T(8,128)(2,1)S(1)} %collective-permute-done.4) | copy-start | bytes 1572868
  81.7 13.5 %collective-permute-start.6 = (bf16[8,32,1024]{2,1,0:T(8,128)(2,1)S(1)}, bf16[8,32,1024]{2,1,0:T(8,128)(2,1)S(1)}, u32[]{:S(2)}, u32[]{:S(2)}) collective-permute-start(bf16[8,32,1024]{2,1,0:T(8,128)(2,1)S(1)} %collective-permute-done.4), channel_id=1, source_target_pairs={{0,1},{1,2},{2,3},{3,4},{4,5},{5,6},{6,7},{7,8},{8,9},{9,10},{10,1... | collective-permute-start | bytes 1572872 | tf_op jit(solution)/shard_map/ppermute | solution.py:96
  81.8 38.2 %copy-start.14 = (bf16[8,32,1024]{2,1,0:T(8,128)(2,1)}, bf16[8,32,1024]{2,1,0:T(8,128)(2,1)S(1)}, u32[]{:S(2)}) copy-start(bf16[8,32,1024]{2,1,0:T(8,128)(2,1)S(1)} %collective-permute-done.5) | copy-start | bytes 1572868
  81.8 13.5 %collective-permute-start.7 = (bf16[8,32,1024]{2,1,0:T(8,128)(2,1)S(1)}, bf16[8,32,1024]{2,1,0:T(8,128)(2,1)S(1)}, u32[]{:S(2)}, u32[]{:S(2)}) collective-permute-start(bf16[8,32,1024]{2,1,0:T(8,128)(2,1)S(1)} %collective-permute-done.5), channel_id=1, source_target_pairs={{0,15},{1,0},{2,1},{3,2},{4,3},{5,4},{6,5},{7,6},{8,7},{9,8},{10,9... | collective-permute-start | bytes 1572872 | tf_op jit(solution)/shard_map/ppermute | solution.py:101
  95.3 24.7 %copy-start.16 = (bf16[8,32,1024]{2,1,0:T(8,128)(2,1)}, bf16[8,32,1024]{2,1,0:T(8,128)(2,1)S(1)}, u32[]{:S(2)}) copy-start(bf16[8,32,1024]{2,1,0:T(8,128)(2,1)S(1)} %collective-permute-done.6) | copy-start | bytes 1572868
  95.3 12.7 %collective-permute-start.8 = (bf16[8,32,1024]{2,1,0:T(8,128)(2,1)S(1)}, bf16[8,32,1024]{2,1,0:T(8,128)(2,1)S(1)}, u32[]{:S(2)}, u32[]{:S(2)}) collective-permute-start(bf16[8,32,1024]{2,1,0:T(8,128)(2,1)S(1)} %collective-permute-done.6), channel_id=1, source_target_pairs={{0,1},{1,2},{2,3},{3,4},{4,5},{5,6},{6,7},{7,8},{8,9},{9,10},{10,1... | collective-permute-start | bytes 1572872 | tf_op jit(solution)/shard_map/ppermute | solution.py:96
  95.3 24.7 %copy-start.18 = (bf16[8,32,1024]{2,1,0:T(8,128)(2,1)}, bf16[8,32,1024]{2,1,0:T(8,128)(2,1)S(1)}, u32[]{:S(2)}) copy-start(bf16[8,32,1024]{2,1,0:T(8,128)(2,1)S(1)} %collective-permute-done.7) | copy-start | bytes 1572868
  95.3 12.7 %collective-permute-start.9 = (bf16[8,32,1024]{2,1,0:T(8,128)(2,1)S(1)}, bf16[8,32,1024]{2,1,0:T(8,128)(2,1)}, u32[]{:S(2)}, u32[]{:S(2)}) collective-permute-start(bf16[8,32,1024]{2,1,0:T(8,128)(2,1)S(1)} %collective-permute-done.7), channel_id=1, source_target_pairs={{0,15},{1,0},{2,1},{3,2},{4,3},{5,4},{6,5},{7,6},{8,7},{9,8},{10,9... | collective-permute-start | bytes 1572872 | tf_op jit(solution)/shard_map/ppermute | solution.py:101
  108.0 12.0 %copy-start.20 = (bf16[8,32,1024]{2,1,0:T(8,128)(2,1)}, bf16[8,32,1024]{2,1,0:T(8,128)(2,1)S(1)}, u32[]{:S(2)}) copy-start(bf16[8,32,1024]{2,1,0:T(8,128)(2,1)S(1)} %collective-permute-done.8) | copy-start | bytes 1572868
  108.0 11.9 %collective-permute-start.10 = (bf16[8,32,1024]{2,1,0:T(8,128)(2,1)S(1)}, bf16[8,32,1024]{2,1,0:T(8,128)(2,1)}, u32[]{:S(2)}, u32[]{:S(2)}) collective-permute-start(bf16[8,32,1024]{2,1,0:T(8,128)(2,1)S(1)} %collective-permute-done.8), channel_id=1, source_target_pairs={{0,1},{1,2},{2,3},{3,4},{4,5},{5,6},{6,7},{7,8},{8,9},{9,10},{10,1... | collective-permute-start | bytes 1572872 | tf_op jit(solution)/shard_map/ppermute | solution.py:96
  108.0 26.1 %collective-permute-start.11 = (bf16[8,32,1024]{2,1,0:T(8,128)(2,1)}, bf16[8,32,1024]{2,1,0:T(8,128)(2,1)}, u32[]{:S(2)}, u32[]{:S(2)}) collective-permute-start(bf16[8,32,1024]{2,1,0:T(8,128)(2,1)} %collective-permute-done.9), channel_id=1, source_target_pairs={{0,15},{1,0},{2,1},{3,2},{4,3},{5,4},{6,5},{7,6},{8,7},{9,8},{10,9... | collective-permute-start | bytes 1572872 | tf_op jit(solution)/shard_map/ppermute | solution.py:101
  120.0 18.9 %collective-permute-start.12 = (bf16[8,32,1024]{2,1,0:T(8,128)(2,1)}, bf16[8,32,1024]{2,1,0:T(8,128)(2,1)S(1)}, u32[]{:S(2)}, u32[]{:S(2)}) collective-permute-start(bf16[8,32,1024]{2,1,0:T(8,128)(2,1)} %collective-permute-done.10), channel_id=1, source_target_pairs={{0,1},{1,2},{2,3},{3,4},{4,5},{5,6},{6,7},{7,8},{8,9},{9,10},{10,1... | collective-permute-start | bytes 1572872 | tf_op jit(solution)/shard_map/ppermute | solution.py:96
  125.6 7.9 %copy-start.2 = (s32[64]{0:T(128)S(1)}, s32[64]{0:T(128)}, u32[]{:S(2)}) copy-start(s32[64]{0:T(128)} %param.11) | copy-start | bytes 772
  134.1 356.5 %collective-permute-start.13 = (bf16[8,32,1024]{2,1,0:T(8,128)(2,1)}, bf16[8,32,1024]{2,1,0:T(8,128)(2,1)}, u32[]{:S(2)}, u32[]{:S(2)}) collective-permute-start(bf16[8,32,1024]{2,1,0:T(8,128)(2,1)} %collective-permute-done.11), channel_id=1, source_target_pairs={{0,15},{1,0},{2,1},{3,2},{4,3},{5,4},{6,5},{7,6},{8,7},{9,8},{10,9... | collective-permute-start | bytes 1572872 | tf_op jit(solution)/shard_map/ppermute | solution.py:101
  138.9 378.1 %collective-permute-start.14 = (bf16[8,32,1024]{2,1,0:T(8,128)(2,1)S(1)}, bf16[8,32,1024]{2,1,0:T(8,128)(2,1)}, u32[]{:S(2)}, u32[]{:S(2)}) collective-permute-start(bf16[8,32,1024]{2,1,0:T(8,128)(2,1)S(1)} %collective-permute-done.12), channel_id=1, source_target_pairs={{0,1},{1,2},{2,3},{3,4},{4,5},{5,6},{6,7},{7,8},{8,9},{9,10},{10,1... | collective-permute-start | bytes 1572872 | tf_op jit(solution)/shard_map/ppermute | solution.py:96
  165.1 25.6 %copy-start.6 = (bf16[8,32,1024]{2,1,0:T(8,128)(2,1)S(1)}, bf16[8,32,1024]{2,1,0:T(8,128)(2,1)}, u32[]{:S(2)}) copy-start(bf16[8,32,1024]{2,1,0:T(8,128)(2,1)} %copy-done.5) | copy-start | bytes 1572868
  192.5 23.8 %copy-start.8 = (bf16[8,32,1024]{2,1,0:T(8,128)(2,1)S(1)}, bf16[8,32,1024]{2,1,0:T(8,128)(2,1)}, u32[]{:S(2)}) copy-start(bf16[8,32,1024]{2,1,0:T(8,128)(2,1)} %copy-done.7) | copy-start | bytes 1572868
  218.0 23.0 %copy-start.11 = (bf16[8,32,1024]{2,1,0:T(8,128)(2,1)S(1)}, bf16[8,32,1024]{2,1,0:T(8,128)(2,1)}, u32[]{:S(2)}) copy-start(bf16[8,32,1024]{2,1,0:T(8,128)(2,1)} %copy-done.10) | copy-start | bytes 1572868
  242.8 23.8 %copy-start.13 = (bf16[8,32,1024]{2,1,0:T(8,128)(2,1)S(1)}, bf16[8,32,1024]{2,1,0:T(8,128)(2,1)}, u32[]{:S(2)}) copy-start(bf16[8,32,1024]{2,1,0:T(8,128)(2,1)} %copy-done.12) | copy-start | bytes 1572868
  268.3 23.0 %copy-start.15 = (bf16[8,32,1024]{2,1,0:T(8,128)(2,1)S(1)}, bf16[8,32,1024]{2,1,0:T(8,128)(2,1)}, u32[]{:S(2)}) copy-start(bf16[8,32,1024]{2,1,0:T(8,128)(2,1)} %copy-done.14) | copy-start | bytes 1572868
  293.1 23.8 %copy-start.17 = (bf16[8,32,1024]{2,1,0:T(8,128)(2,1)S(1)}, bf16[8,32,1024]{2,1,0:T(8,128)(2,1)}, u32[]{:S(2)}) copy-start(bf16[8,32,1024]{2,1,0:T(8,128)(2,1)} %copy-done.16) | copy-start | bytes 1572868
  318.6 19.6 %copy-start.19 = (bf16[8,32,1024]{2,1,0:T(8,128)(2,1)S(1)}, bf16[8,32,1024]{2,1,0:T(8,128)(2,1)}, u32[]{:S(2)}) copy-start(bf16[8,32,1024]{2,1,0:T(8,128)(2,1)} %copy-done.18) | copy-start | bytes 1572868
  340.0 20.5 %copy-start.21 = (bf16[8,32,1024]{2,1,0:T(8,128)(2,1)S(1)}, bf16[8,32,1024]{2,1,0:T(8,128)(2,1)}, u32[]{:S(2)}) copy-start(bf16[8,32,1024]{2,1,0:T(8,128)(2,1)} %copy-done.20) | copy-start | bytes 1572868
  692.0 20.3 %all-to-all-start.1 = ((f32[8,32,1024]{2,1,0:T(8,128)}), f32[8,32,1024]{2,1,0:T(8,128)}, u32[]{:S(2)}, u32[]{:S(2)}) async-start(f32[8,32,1024]{2,1,0:T(8,128)} %broadcast_select_fusion), calls=%async_computation.2 | async-start | bytes 2097152 | tf_op jit(solution)/shard_map/all_to_all | solution.py:110
  714.2 2.3 copy-start.3
Sparse Core Ops, SparseCore 0:
  571.9 117.0 reduce-scatter.1
